TPU v7x, 32 devices: a whole 2x2x4 slice. The times are simulated.
32 devices in a mesh: layer: 2 (over x), row: 4 (over y, core), col: 4 (over z).
Axes of the slice: x: 2, y: 2, z: 4, core: 2. Of those that a mesh axis runs over, the one named last changes fastest.
Arguments:
- left_matrix: bfloat16 [8192, 1024], P('row', ('layer', 'col')), may hold values from -6 to 6
- square_term: bfloat16 [1024, 1024], P(('layer', 'row'), 'col'), may hold values from -0.5 to 0.5
- block_pattern: int32 [64, 8], replicated, may hold values from 0 to 1, as said below
- keep_mask: int32 [64, 8], replicated, may hold values 0 or 1
Outputs:
- product: bfloat16 [8192, 1024], P('row', 'col')
Inputs may be any that keep to these rules, and one draw needn't show every extreme that they name: `block_pattern`: in each aligned group of 16 block rows, every block column holds 1 to 8 stored blocks; some group holds exactly 8.
All inputs are finite; a program needn't handle non-finite values.
Results may differ from a plain program's by a relative error of at most 0.0038.
Values may be sent and summed in bfloat16 or wider, within the bound.
No kernel may reach another device: no remote copies, remote signals or barrier semaphores. Data moves between devices by JAX's collectives and lax.ppermute only.
A program may use at most 64 MiB of HBM per device.

v0:
```python
import jax
import jax.numpy as jnp
from jax import lax
from jax.sharding import PartitionSpec as P

BLK = 128


def expand(mask_blocks):
    return jnp.repeat(jnp.repeat(mask_blocks, BLK, axis=0), BLK, axis=1)


def per_device(left_matrix, square_term, block_pattern, keep_mask):
    row_idx = lax.axis_index("row")
    col_idx = lax.axis_index("col")
    layer_idx = lax.axis_index("layer")
    row_count = lax.axis_size("row")
    col_count = lax.axis_size("col")
    rows_local = left_matrix.shape[0]
    row_blocks = rows_local // BLK
    inner_blocks = left_matrix.shape[1] // BLK
    inner_local = square_term.shape[0]
    cols_local = square_term.shape[1]
    col_blocks = cols_local // BLK
    inner_start = (layer_idx * col_count + col_idx) * inner_blocks
    pattern_patch = lax.dynamic_slice(
        block_pattern, (row_idx * row_blocks, inner_start), (row_blocks, inner_blocks)
    )
    first_inner = (layer_idx * row_count + row_idx) * inner_local
    first_col = col_idx * cols_local
    inner_pos = first_inner + lax.broadcasted_iota(jnp.int32, (inner_local, cols_local), 0)
    col_pos = first_col + lax.broadcasted_iota(jnp.int32, (inner_local, cols_local), 1)
    unit = jnp.where(inner_pos == col_pos, jnp.float32(1.5), jnp.float32(0.0))
    right_factor = (unit - 0.5 * square_term.astype(jnp.float32)).astype(jnp.bfloat16)
    right_half = lax.all_gather(right_factor, "row", axis=0, tiled=True)
    sparse_left = jnp.where(expand(pattern_patch) > 0, left_matrix, jnp.zeros_like(left_matrix))
    partial_sum = jnp.dot(
        lax.all_gather(sparse_left, "col", axis=1, tiled=True),
        right_half,
        preferred_element_type=jnp.float32,
    )
    keep_patch = lax.dynamic_slice(
        keep_mask, (row_idx * row_blocks, col_idx * col_blocks), (row_blocks, col_blocks)
    )
    keep_full = expand(keep_patch)
    full_sum = lax.psum(partial_sum, "layer")
    kept = jnp.where(keep_full > 0, full_sum, jnp.zeros_like(full_sum))
    return kept.astype(jnp.bfloat16)


def solution(mesh):
    return jax.shard_map(
        per_device,
        mesh=mesh,
        in_specs=(P("row", ("layer", "col")), P(("layer", "row"), "col"), P(), P()),
        out_specs=P("row", "col"),
        check_vma=False,
    )
```

profile of v0, /device:TPU:0, one launch (start us, length us, event | category | flops | bytes accessed | tf_op | source)
XLA Modules:
  0.0 123.4 jit_solution(1267802918335464349)
XLA Ops:
  6.5 0.0 copy-start
  6.5 0.0 all-gather.2.cloned.1.call-start
  6.5 0.8 compare_bitcast_fusion
  7.3 0.1 broadcast_bitcast_fusion.1
  7.4 2.2 %broadcast_select_fusion = bf16[2048,128]{1,0:T(8,128)(2,1)} fusion(bf16[2048,128]{1,0:T(8,128)(2,1)} %param.4, pred[2048]{0:T(1024)(128)(4,1)S(1)} %broadcast_bitcast_fusion.1), kind=kLoop, calls=%fused_computation.1 | loop fusion | flops 262144 | bytes 1050624 | tf_op jit(solution)/shard_map/jit(_where)/select_n | solution.py:36
  9.6 0.0 all-gather.2.cloned.1.call-update
  9.6 0.8 dynamic-slice_compare_fusion
  10.4 0.1 broadcast_bitcast_fusion
  10.5 0.2 broadcast_in_dim.25
  10.7 1.5 %copy.6 = pred[2048,256]{1,0:T(8,128)(4,1)} copy(pred[2048,256]{0,1:T(8,128)(4,1)S(1)} %bitcast.14) | data formatting | bytes 1048576 | tf_op jit(solution)/shard_map/gt | solution.py:47
  12.2 0.0 copy-done
  12.2 0.1 subtract_convert_fusion
  12.3 7.2 %all_gather.7 = bf16[512,256]{1,0:T(8,128)(2,1)S(1)} all-gather(bf16[128,256]{1,0:T(8,128)(2,1)S(1)} %subtract_convert_fusion), channel_id=1, replica_groups=mesh['layer'=2,'row'=4,'col'=4] {'row'}, dimensions={0}, use_global_device_ids=true | all-gather | bytes 327680 | tf_op jit(solution)/shard_map/all_gather | solution.py:35
  19.5 39.2 %all-gather.2.cloned.1.call-done = bf16[2048,512]{1,0:T(8,128)(2,1)} async-done(((bf16[2048,128]{1,0:T(8,128)(2,1)}), bf16[2048,512]{1,0:T(8,128)(2,1)}) %all-gather.2.cloned.1.call-update) | async-done | bytes 2097168 | tf_op jit(solution)/shard_map/all_gather | solution.py:38
  58.7 2.3 %fusion = f32[2048,256]{1,0:T(8,128)S(1)} fusion(bf16[2048,512]{1,0:T(8,128)(2,1)} %all-gather.2.cloned.1.call-done, bf16[512,256]{1,0:T(8,128)(2,1)S(1)} %all_gather.7), kind=kOutput, calls=%fused_computation.10 | convolution fusion | flops 536870912 | bytes 4456448 | tf_op jit(solution)/shard_map/dot_general | solution.py:37
  61.0 53.2 %all-reduce.1 = bf16[2048,256]{1,0:T(8,128)(2,1)S(1)} all-reduce(f32[2048,256]{1,0:T(8,128)S(1)} %fusion), channel_id=1, replica_groups=mesh['layer'=2,'row'=4,'col'=4] {'layer'}, use_global_device_ids=true, to_apply=%region_0.1 | all-reduce | flops 524288 | bytes 3145728 | tf_op jit(solution)/shard_map/psum | solution.py:46
  114.2 2.3 %select_convert_fusion = bf16[2048,256]{1,0:T(8,128)(2,1)} fusion(pred[2048,256]{1,0:T(8,128)(4,1)} %copy.6, bf16[2048,256]{1,0:T(8,128)(2,1)S(1)} %all-reduce.1), kind=kLoop, calls=%fused_computation | loop fusion | flops 524288 | bytes 2621440 | tf_op jit(solution)/shard_map/convert_element_type | solution.py:48
  (3 shorter events, 0.0 us)
Async XLA Ops:
  6.5 5.6 %copy-start = (bf16[128,256]{1,0:T(8,128)(2,1)S(1)}, bf16[128,256]{1,0:T(8,128)(2,1)}, u32[]{:S(2)}) copy-start(bf16[128,256]{1,0:T(8,128)(2,1)} %param.5) | copy-start | bytes 196612
  6.5 52.2 %all-gather.2.cloned.1.call-start = ((), (), s32[]{:S(2)}) async-start(), calls=%async_computation | async-start | bytes 2621440 | tf_op jit(solution)/shard_map/all_gather | solution.py:38
Sparse Core Ops, SparseCore 0:
  9.7 48.9 all-gather.1
where the time goes:
time: 124 us; the launch traced here: 123 us
  blocking collectives  60.4 us (49%)
  waiting for transfers between devices  39.2 us (32%)
  between operations  13.4 us (11%)
  other arithmetic  6.15 us (5%)
  matrix products  2.29 us (2%)
  local copies, waits for them, and re-layouts  1.83 us (1%)
    psum x1, blocking collectives, per_device(): full_sum = lax.psum(partial_sum, 'layer')  53.2 us
    all_gather x1, waiting for transfers between devices, per_device(): lax.all_gather(sparse_left, 'col', axis=1, tiled=True)  39.2 us
    all_gather x1, blocking collectives, per_device(): right_half = lax.all_gather(right_factor, 'row', axis=0, tiled=True)  7.22 us
  transfers between devices with their start and end apart: 1, of which 1 were waited for; matrix products, arithmetic and copies ran while one was open for 2% of the time, Pallas kernels for 0%

commit v1 on v0

--- a/solution.py
+++ b/solution.py
@@ -4,6 +4,17 @@
 from jax.sharding import PartitionSpec as P
 
 BLK = 128
+
+
+def gather_by_hops(value, mesh_axis, dim):
+    size = lax.axis_size(mesh_axis)
+    hops = [(i, (i + 1) % size) for i in range(size)]
+    blocks = [value]
+    for far in range(1, size):
+        blocks = [lax.ppermute(blocks[0], mesh_axis, hops), *blocks]
+    whole = jnp.concatenate(blocks, axis=dim)
+    shift = (lax.axis_index(mesh_axis) + 1) * blocks[-1].shape[dim]
+    return jnp.roll(whole, shift, axis=dim)
 
 
 def expand(mask_blocks):
@@ -32,7 +43,7 @@
     col_pos = first_col + lax.broadcasted_iota(jnp.int32, (inner_local, cols_local), 1)
     unit = jnp.where(inner_pos == col_pos, jnp.float32(1.5), jnp.float32(0.0))
     right_factor = (unit - 0.5 * square_term.astype(jnp.float32)).astype(jnp.bfloat16)
-    right_half = lax.all_gather(right_factor, "row", axis=0, tiled=True)
+    right_half = gather_by_hops(right_factor, "row", 0)
     sparse_left = jnp.where(expand(pattern_patch) > 0, left_matrix, jnp.zeros_like(left_matrix))
     partial_sum = jnp.dot(
         lax.all_gather(sparse_left, "col", axis=1, tiled=True),

time: 124 us -> 124 us (level)
  blocking collectives: 60.4 us -> 53.2 us
  waiting for transfers between devices: 39.2 us -> 44.8 us
    ppermute x0 -> x3, waiting for transfers between devices: none -> 8.66 us  [gather_by_hops(): blocks = [lax.ppermute(blocks[0], mesh_axis, hops), *blocks]]
    all_gather x1 -> x0, blocking collectives: 7.22 us -> none  [per_device(): right_half = lax.all_gather(right_factor, 'row', axis=0, tiled=True)]
    all_gather x1, waiting for transfers between devices: 39.2 us -> 36.1 us  [per_device(): lax.all_gather(sparse_left, 'col', axis=1, tiled=True)]
  transfers between devices with their start and end apart: 1 -> 4, of which waited for: 1 -> 4; matrix products, arithmetic and copies ran while one was open for 2% -> 3% of each run, Pallas kernels for 0% -> 0%
where the time goes in v1:
time: 124 us; the launch traced here: 123 us
  blocking collectives  53.2 us (43%)
  waiting for transfers between devices  44.8 us (36%)
  between operations  13.5 us (11%)
  other arithmetic  7.16 us (6%)
  matrix products  2.3 us (2%)
  local copies, waits for them, and re-layouts  1.85 us (1%)
    psum x1, blocking collectives, per_device(): full_sum = lax.psum(partial_sum, 'layer')  53.2 us
    all_gather x1, waiting for transfers between devices, per_device(): lax.all_gather(sparse_left, 'col', axis=1, tiled=True)  36.1 us
    ppermute x3, waiting for transfers between devices, gather_by_hops(): blocks = [lax.ppermute(blocks[0], mesh_axis, hops), *blocks]  8.66 us
  transfers between devices with their start and end apart: 4, of which 4 were waited for; matrix products, arithmetic and copies ran while one was open for 3% of the time, Pallas kernels for 0%

profile of v1, /device:TPU:0, one launch (start us, length us, event | category | flops | bytes accessed | tf_op | source)
XLA Modules:
  0.0 123.4 jit_solution(15491808068265470410)
XLA Ops:
  6.5 0.0 copy-start
  6.5 0.0 all-gather.2.cloned.1.call-start
  6.5 0.8 compare_bitcast_fusion
  7.3 0.1 broadcast_bitcast_fusion.1
  7.4 2.2 %broadcast_select_fusion = bf16[2048,128]{1,0:T(8,128)(2,1)} fusion(bf16[2048,128]{1,0:T(8,128)(2,1)} %param.4, pred[2048]{0:T(1024)(128)(4,1)S(1)} %broadcast_bitcast_fusion.1), kind=kLoop, calls=%fused_computation.1 | loop fusion | flops 262144 | bytes 1050624 | tf_op jit(solution)/shard_map/jit(_where)/select_n | solution.py:47
  9.6 0.0 all-gather.2.cloned.1.call-update
  9.6 0.9 subtract_convert_fusion
  10.6 0.5 collective-permute-start
  11.1 3.9 %collective-permute-done = bf16[128,256]{1,0:T(8,128)(2,1)S(1)} collective-permute-done((bf16[128,256]{1,0:T(8,128)(2,1)S(1)}, bf16[128,256]{1,0:T(8,128)(2,1)S(1)}, u32[]{:S(2)}, u32[]{:S(2)}) %collective-permute-start) | collective-permute-done | bytes 65568 | tf_op jit(solution)/shard_map/ppermute | solution.py:14
  15.0 0.1 collective-permute-start.1
  15.0 0.8 dynamic-slice_compare_fusion
  15.8 2.9 %collective-permute-done.1 = bf16[128,256]{1,0:T(8,128)(2,1)S(1)} collective-permute-done((bf16[128,256]{1,0:T(8,128)(2,1)S(1)}, bf16[128,256]{1,0:T(8,128)(2,1)S(1)}, u32[]{:S(2)}, u32[]{:S(2)}) %collective-permute-start.1) | collective-permute-done | bytes 65568 | tf_op jit(solution)/shard_map/ppermute | solution.py:14
  18.7 0.1 collective-permute-start.2
  18.7 0.1 broadcast_bitcast_fusion
  18.8 0.2 broadcast_in_dim.25
  19.0 1.4 %copy.6 = pred[2048,256]{1,0:T(8,128)(4,1)} copy(pred[2048,256]{0,1:T(8,128)(4,1)S(1)} %bitcast.13) | data formatting | bytes 1048576 | tf_op jit(solution)/shard_map/gt | solution.py:58
  20.5 1.9 %collective-permute-done.2 = bf16[128,256]{1,0:T(8,128)(2,1)S(1)} collective-permute-done((bf16[128,256]{1,0:T(8,128)(2,1)S(1)}, bf16[128,256]{1,0:T(8,128)(2,1)S(1)}, u32[]{:S(2)}, u32[]{:S(2)}) %collective-permute-start.2) | collective-permute-done | bytes 65568 | tf_op jit(solution)/shard_map/ppermute | solution.py:14
  22.4 0.0 copy-done
  22.4 0.1 constant_dynamic-update-slice_fusion.4
  22.5 0.1 constant_dynamic-update-slice_fusion
  22.6 36.1 %all-gather.2.cloned.1.call-done = bf16[2048,512]{1,0:T(8,128)(2,1)} async-done(((bf16[2048,128]{1,0:T(8,128)(2,1)}), bf16[2048,512]{1,0:T(8,128)(2,1)}) %all-gather.2.cloned.1.call-update) | async-done | bytes 2097168 | tf_op jit(solution)/shard_map/all_gather | solution.py:49
  58.8 2.3 %fusion = f32[2048,256]{1,0:T(8,128)S(1)} fusion(bf16[2048,512]{1,0:T(8,128)(2,1)} %all-gather.2.cloned.1.call-done, bf16[1024,256]{1,0:T(8,128)(2,1)S(1)} %constant_dynamic-update-slice_fusion, s32[]{:T(128)S(6)} %select_n.41), kind=kOutput, calls=%fused_computation.2 | convolution fusion | flops 536870912 | bytes 4456452 | tf_op jit(solution)/shard_map/dot_general | solution.py:48
  61.1 53.2 %all-reduce.1 = bf16[2048,256]{1,0:T(8,128)(2,1)S(1)} all-reduce(f32[2048,256]{1,0:T(8,128)S(1)} %fusion), channel_id=1, replica_groups=mesh['layer'=2,'row'=4,'col'=4] {'layer'}, use_global_device_ids=true, to_apply=%region_0.1 | all-reduce | flops 524288 | bytes 3145728 | tf_op jit(solution)/shard_map/psum | solution.py:57
  114.2 2.3 %select_convert_fusion = bf16[2048,256]{1,0:T(8,128)(2,1)} fusion(pred[2048,256]{1,0:T(8,128)(4,1)} %copy.6, bf16[2048,256]{1,0:T(8,128)(2,1)S(1)} %all-reduce.1), kind=kLoop, calls=%fused_computation | loop fusion | flops 524288 | bytes 2621440 | tf_op jit(solution)/shard_map/convert_element_type | solution.py:59
  (9 shorter events, 0.1 us)
Async XLA Ops:
  6.5 15.9 %copy-start = (bf16[128,256]{1,0:T(8,128)(2,1)S(1)}, bf16[128,256]{1,0:T(8,128)(2,1)}, u32[]{:S(2)}) copy-start(bf16[128,256]{1,0:T(8,128)(2,1)} %param.5) | copy-start | bytes 196612
  6.5 52.2 %all-gather.2.cloned.1.call-start = ((), (), s32[]{:S(2)}) async-start(), calls=%async_computation | async-start | bytes 2621440 | tf_op jit(solution)/shard_map/all_gather | solution.py:49
  10.6 4.4 %collective-permute-start = (bf16[128,256]{1,0:T(8,128)(2,1)S(1)}, bf16[128,256]{1,0:T(8,128)(2,1)S(1)}, u32[]{:S(2)}, u32[]{:S(2)}) collective-permute-start(bf16[128,256]{1,0:T(8,128)(2,1)S(1)} %subtract_convert_fusion), channel_id=1, source_target_pairs={{0,4},{4,8},{8,12},{12,0},{1,5},{5,9},{9,13},{13,1},{2,6},{6,10},{... | collective-permute-start | bytes 196616 | tf_op jit(solution)/shard_map/ppermute | solution.py:14
  15.0 3.7 %collective-permute-start.1 = (bf16[128,256]{1,0:T(8,128)(2,1)S(1)}, bf16[128,256]{1,0:T(8,128)(2,1)S(1)}, u32[]{:S(2)}, u32[]{:S(2)}) collective-permute-start(bf16[128,256]{1,0:T(8,128)(2,1)S(1)} %collective-permute-done), channel_id=1, source_target_pairs={{0,4},{4,8},{8,12},{12,0},{1,5},{5,9},{9,13},{13,1},{2,6},{6,10},{... | collective-permute-start | bytes 196616 | tf_op jit(solution)/shard_map/ppermute | solution.py:14
  18.7 3.7 %collective-permute-start.2 = (bf16[128,256]{1,0:T(8,128)(2,1)S(1)}, bf16[128,256]{1,0:T(8,128)(2,1)S(1)}, u32[]{:S(2)}, u32[]{:S(2)}) collective-permute-start(bf16[128,256]{1,0:T(8,128)(2,1)S(1)} %collective-permute-done.1), channel_id=1, source_target_pairs={{0,4},{4,8},{8,12},{12,0},{1,5},{5,9},{9,13},{13,1},{2,6},{6,10},{... | collective-permute-start | bytes 196616 | tf_op jit(solution)/shard_map/ppermute | solution.py:14
Sparse Core Ops, SparseCore 0:
  9.7 48.9 all-gather.1
